TPU v7x, 128 devices: a whole 4x4x4 slice. The times are simulated.
128 devices in a mesh: dp: 8 (over x, core), tensor: 16 (over z, y).
Axes of the slice: x: 4, y: 4, z: 4, core: 2. Of those that a mesh axis runs over, the one named last changes fastest.
Arguments:
- hidden: bfloat16 [2048, 8192], P('dp', 'tensor'), may hold values from -170 to 170, as said below
- neighbour_ids: int32 [32, 2], P('dp'), may hold values from 0 to 255, as said below
- database: bfloat16 [256, 128, 8192], P('dp', None, 'tensor'), may hold values from -6 to 6
- w_query: bfloat16 [8192, 4096], P(None, 'tensor'), may hold values from -0.0625 to 0.0625
- w_key: bfloat16 [8192, 4096], P(None, 'tensor'), may hold values from -0.0625 to 0.0625
- w_value: bfloat16 [8192, 4096], P(None, 'tensor'), may hold values from -0.0625 to 0.0625
- w_out: bfloat16 [4096, 8192], P('tensor'), may hold values from -0.09375 to 0.09375
Outputs:
- mixed: bfloat16 [2048, 8192], P('dp', 'tensor')
Inputs may be any that keep to these rules, and one draw needn't show every extreme that they name: `neighbour_ids`: database block b is held by index b // 32 of dp. Among the 8 neighbour ids of one sequence (the rows of one device), at most 4 belong to the same holder, and in every sequence exactly 4 do. `hidden`: hidden states may be large for some tokens.
All inputs are finite; a program needn't handle non-finite values.
Results may differ from a plain program's by a relative error of at most 0.02.
Values may be sent and summed in bfloat16 or wider, within the bound.
No kernel may reach another device: no remote copies, remote signals or barrier semaphores. Data moves between devices by JAX's collectives and lax.ppermute only.
A program may use at most 128 MiB of HBM per device.

v0:
```python
import jax
import jax.numpy as jnp
from jax import lax
from jax.sharding import PartitionSpec as P

HD = 128


def attend(query_rows, key_rows, value_rows, heads_count, group_len):
    tok_count, width = query_rows.shape
    groups = tok_count // group_len
    head_size = width // heads_count
    shifted = jnp.concatenate(
        [query_rows[group_len - 1 :], jnp.zeros((group_len - 1, width), jnp.bfloat16)], 0
    )
    shifted = shifted.reshape(groups, group_len, heads_count, head_size)
    key_block = key_rows.reshape(groups, -1, heads_count, head_size)
    value_block = value_rows.reshape(groups, -1, heads_count, head_size)
    scores = jnp.einsum(
        "cqhd,ckhd->chqk", shifted, key_block, preferred_element_type=jnp.float32
    ) / jnp.sqrt(jnp.float32(head_size))
    top_score = jnp.max(scores, axis=-1, keepdims=True)
    weights_raw = jnp.exp(scores - top_score)
    soft = (weights_raw / jnp.sum(weights_raw, axis=-1, keepdims=True)).astype(jnp.bfloat16)
    blended = jnp.einsum(
        "chqk,ckhd->cqhd", soft, value_block, preferred_element_type=jnp.float32
    ).astype(jnp.bfloat16)
    blended = blended.reshape(tok_count, width)
    return jnp.concatenate(
        [jnp.zeros((group_len - 1, width), jnp.bfloat16), blended[: tok_count - group_len + 1]], 0
    )


def shards(hidden, neighbour_ids, database, w_query, w_key, w_value, w_out):
    dp_count = lax.axis_size("dp")
    tok_rows = hidden.shape[0]
    group_count = neighbour_ids.shape[0]
    per_reader = group_count * neighbour_ids.shape[1]
    capacity = per_reader // 2
    db_count = database.shape[0]
    ret_len = database.shape[1]
    col_count = database.shape[2]
    head_cols = w_query.shape[1]
    heads_local = head_cols // HD
    query_sum = jnp.dot(
        lax.all_gather(hidden, "tensor", axis=1, tiled=True),
        w_query,
        preferred_element_type=jnp.float32,
    )
    query_rows = query_sum.astype(jnp.bfloat16)
    block_ids = neighbour_ids.reshape(per_reader)
    owners = block_ids // db_count
    earlier = jnp.arange(per_reader)[:, None] > jnp.arange(per_reader)[None, :]
    slot_rank = jnp.sum(((owners[:, None] == owners[None, :]) & earlier).astype(jnp.int32), 1)
    slot_range = jnp.arange(capacity, dtype=jnp.int32)
    local_index = block_ids % db_count
    owner_range = jnp.arange(dp_count, dtype=jnp.int32)
    slot_hit = (owners[:, None, None] == owner_range[None, :, None]) & (
        slot_rank[:, None, None] == slot_range[None, None, :]
    )
    request_table = jnp.sum(slot_hit.astype(jnp.int32) * local_index[:, None, None], 0)
    requested = lax.all_to_all(request_table, "dp", split_axis=0, concat_axis=0, tiled=True)
    outgoing = jnp.take(database, requested.reshape(-1), axis=0).reshape(
        dp_count, capacity, ret_len, col_count
    )
    arrived = lax.all_to_all(outgoing, "dp", split_axis=0, concat_axis=0, tiled=True)
    neighbour_rows = jnp.take(
        arrived.reshape(dp_count * capacity, ret_len, col_count),
        owners * capacity + slot_rank,
        axis=0,
    )
    assembled = lax.all_gather(neighbour_rows, "tensor", axis=2, tiled=True).reshape(
        per_reader * ret_len, -1
    )
    key_sum = jnp.dot(assembled, w_key, preferred_element_type=jnp.float32)
    value_sum = jnp.dot(assembled, w_value, preferred_element_type=jnp.float32)
    key_rows = key_sum.astype(jnp.bfloat16)
    value_rows = value_sum.astype(jnp.bfloat16)
    group_len = tok_rows // group_count
    context = attend(query_rows, key_rows, value_rows, heads_local, group_len)
    live = context[group_len - 1 :]
    live_rows = live.shape[0]
    tensor_count = lax.axis_size("tensor")
    partial_out = jnp.dot(live, w_out, preferred_element_type=jnp.float32).astype(jnp.bfloat16)
    spread = lax.all_to_all(
        partial_out.reshape(live_rows, tensor_count, -1),
        "tensor",
        split_axis=1,
        concat_axis=1,
        tiled=True,
    )
    summed = jnp.sum(spread.astype(jnp.float32), axis=1).astype(jnp.bfloat16)
    return jnp.concatenate([jnp.zeros((group_len - 1, summed.shape[1]), jnp.bfloat16), summed], 0)


def solution(mesh):
    placed = (
        P("dp", "tensor"),
        P("dp", None),
        P("dp", None, "tensor"),
        P(None, "tensor"),
        P(None, "tensor"),
        P(None, "tensor"),
        P("tensor", None),
    )
    return jax.shard_map(
        shards, mesh=mesh, in_specs=placed, out_specs=P("dp", "tensor"), check_vma=False
    )
```

profile of v0, /device:TPU:0, one launch (start us, length us, event | category | flops | bytes accessed | tf_op | source)
XLA Modules:
  0.0 293.9 jit_solution(2541385137041955387)
XLA Ops:
  6.5 0.0 all-gather.5.cloned.1.call-start
  6.5 0.7 all-gather.5.cloned.1.call-update
  7.3 0.8 copy.33
  8.0 0.1 reshape.302
  8.1 0.2 convert_reduce_fusion
  8.3 0.1 iota_compare_fusion
  8.4 0.1 select_reduce_fusion
  8.5 0.1 copy.34
  8.6 9.5 %all_to_all.19 = s32[8,1,4]{2,1,0:T(1,128)S(1)} all-to-all(s32[8,1,4]{2,1,0:T(1,128)S(1)} %copy.34), channel_id=1, replica_groups=mesh['dp'=8,'tensor'=16] {'dp'}, dimensions={0} | all-to-all | bytes 256 | tf_op jit(solution)/shard_map/all_to_all | solution.py:62
  18.1 0.5 broadcast.311
  18.6 0.7 reduce.4
  19.2 0.1 reshape.304
  19.3 0.1 copy.35
  19.4 0.1 copy.36
  19.5 5.1 %gather_fusion = bf16[32,128,512]{2,1,0:T(8,128)(2,1)} fusion(bf16[32,128,512]{2,1,0:T(8,128)(2,1)} %param.9, s32[1024]{0:T(1024)S(1)} %pad_clamp_fusion.1), kind=kCustom, calls=%fused_computation | custom fusion | bytes 8388736 | tf_op jit(solution)/shard_map/jit(_take)/gather | solution.py:63
  24.6 4.6 %broadcast_select_fusion = bf16[8,4,128,512]{3,2,1,0:T(8,128)(2,1)} fusion(bf16[8,4,128,512]{3,2,1,0:T(8,128)(2,1)} %bitcast.36, pred[8,4]{1,0:T(8,128)(4,1)S(1)} %copy.36), kind=kLoop, calls=%fused_computation.4 | loop fusion | flops 2097152 | bytes 8388640 | tf_op jit(solution)/shard_map/jit(_take)/select_n | solution.py:63
  29.2 4.6 %all-to-all-start.1 = ((bf16[8,4,128,512]{3,2,1,0:T(8,128)(2,1)}), bf16[8,4,128,512]{3,2,1,0:T(8,128)(2,1)}, u32[]{:S(2)}, u32[]{:S(2)}) async-start(bf16[8,4,128,512]{3,2,1,0:T(8,128)(2,1)} %broadcast_select_fusion), calls=%async_computation.1 | async-start | bytes 8388608 | tf_op jit(solution)/shard_map/all_to_all | solution.py:66
  33.7 0.0 all-gather.3.cloned.1.call-start
  33.8 0.1 reshape.306
  33.9 49.5 %all-to-all-done.1 = bf16[8,4,128,512]{3,2,1,0:T(8,128)(2,1)} async-done(((bf16[8,4,128,512]{3,2,1,0:T(8,128)(2,1)}), bf16[8,4,128,512]{3,2,1,0:T(8,128)(2,1)}, u32[]{:S(2)}, u32[]{:S(2)}) %all-to-all-start.1) | async-done | bytes 4194336 | tf_op jit(solution)/shard_map/all_to_all | solution.py:66
  83.4 2.8 gather_fusion.1
  86.2 1.1 broadcast_select_fusion.1
  87.3 0.0 all-gather.3.cloned.1.call-update
  87.3 0.0 all-gather.5.cloned.1.call-done
  87.4 4.7 %fusion.14 = bf16[256,256]{1,0:T(8,128)(2,1)S(1)} fusion(bf16[256,8192]{1,0:T(8,128)(2,1)} %all-gather.5.cloned.1.call-done, bf16[8192,256]{1,0:T(8,128)(2,1)} %param.10), kind=kOutput, calls=%fused_computation.49 | convolution fusion | flops 1073741824 | bytes 8519680 | tf_op jit(solution)/shard_map/dot_general | solution.py:45
  92.2 115.9 %all-gather.3.cloned.1.call-done = bf16[8,128,8192]{2,1,0:T(8,128)(2,1)} async-done(((bf16[8,128,512]{2,1,0:T(8,128)(2,1)}), bf16[8,128,8192]{2,1,0:T(8,128)(2,1)}) %all-gather.3.cloned.1.call-update) | async-done | bytes 16777232 | tf_op jit(solution)/shard_map/all_gather | solution.py:72
  208.1 11.4 %convolution_convert_fusion.2 = bf16[1024,256]{1,0:T(8,128)(2,1)S(1)} fusion(bf16[1024,8192]{1,0:T(8,128)(2,1)} %bitcast.41, bf16[8192,256]{1,0:T(8,128)(2,1)} %param.12), kind=kOutput, calls=%fused_computation.6 | convolution fusion | flops 4295229440 | bytes 21495808 | tf_op jit(solution)/shard_map/dot_general | solution.py:76
  219.6 0.1 reshape.308
  219.7 11.4 %convolution_convert_fusion.1 = bf16[1024,256]{1,0:T(8,128)(2,1)S(1)} fusion(bf16[1024,8192]{1,0:T(8,128)(2,1)} %bitcast.42, bf16[8192,256]{1,0:T(8,128)(2,1)} %param.11), kind=kOutput, calls=%fused_computation.5 | convolution fusion | flops 4295229440 | bytes 21495808 | tf_op jit(solution)/shard_map/dot_general | solution.py:75
  231.1 0.1 reshape.310
  231.3 0.3 convolution_multiply_fusion
  231.6 0.3 fusion.13
  231.8 1.0 fusion.3
  232.8 0.1 copy.41
  233.0 3.2 %convolution_convert_fusion = bf16[193,8192]{1,0:T(8,128)(2,1)S(1)} fusion(bf16[256,8192]{1,0:T(8,128)(2,1)} %param.13, bf16[256,256]{1,0:T(8,128)(2,1)S(1)} %bitcast.38), kind=kOutput, calls=%fused_computation.3 | convolution fusion | flops 811081728 | bytes 7458816 | tf_op jit(solution)/shard_map/dot_general | solution.py:84
  236.2 1.6 copy.44
  237.8 0.3 slice.14
  238.2 1.8 copy.42
  239.9 45.8 %all_to_all.20 = bf16[193,16,512]{2,0,1:T(8,128)(2,1)S(1)} all-to-all(bf16[193,16,512]{2,0,1:T(8,128)(2,1)S(1)} %copy.42), channel_id=1, replica_groups=mesh['dp'=8,'tensor'=16] {'tensor'}, dimensions={1} | all-to-all | bytes 6324224 | tf_op jit(solution)/shard_map/all_to_all | solution.py:85
  285.7 0.5 reduce_sum.45
  286.3 0.8 concatenate.7
  (12 shorter events, 0.2 us)
Async XLA Ops:
  6.5 80.8 %all-gather.5.cloned.1.call-start = ((), (), s32[]{:S(2)}) async-start(), calls=%async_computation.4 | async-start | bytes 4456448 | tf_op jit(solution)/shard_map/all_gather | solution.py:46
  29.2 54.2 %all-to-all-start.1 = ((bf16[8,4,128,512]{3,2,1,0:T(8,128)(2,1)}), bf16[8,4,128,512]{3,2,1,0:T(8,128)(2,1)}, u32[]{:S(2)}, u32[]{:S(2)}) async-start(bf16[8,4,128,512]{3,2,1,0:T(8,128)(2,1)} %broadcast_select_fusion), calls=%async_computation.1 | async-start | bytes 8388608 | tf_op jit(solution)/shard_map/all_to_all | solution.py:66
  33.7 174.4 %all-gather.3.cloned.1.call-start = ((), (), s32[]{:S(2)}) async-start(), calls=%async_computation.3 | async-start | bytes 17825792 | tf_op jit(solution)/shard_map/all_gather | solution.py:72
Sparse Core Ops, SparseCore 0:
  9.4 59.4 all-gather.4
  87.5 120.6 all-gather.2
where the time goes:
time: 294 us
  waiting for transfers between devices  166 us (56%)
  blocking collectives  55.3 us (19%)
  matrix products  32.1 us (11%)
  local copies, waits for them, and re-layouts  14.6 us (5%)
  between operations  13.6 us (5%)
  other arithmetic  7.61 us (3%)
  starting transfers between devices  4.6 us (2%)
    all_gather x1, waiting for transfers between devices, shards(): lax.all_gather(neighbour_rows, 'tensor', axis=2, tiled=True)  116 us
    all_to_all x1, waiting for transfers between devices, shards(): lax.all_to_all(outgoing, 'dp', split_axis=0, concat_axis=0, tiled=True)  49.5 us
    all_to_all x1, blocking collectives, shards(): lax.all_to_all(partial_out.reshape(live_rows, tensor_count, -1), 'tensor'...  45.8 us
    dot_general x1, matrix products, shards(): value_sum = jnp.dot(assembled, w_value, preferred_element_type=jnp.float32)  11.4 us
    dot_general x1, matrix products, shards(): key_sum = jnp.dot(assembled, w_key, preferred_element_type=jnp.float32)  11.4 us
    all_to_all x1, blocking collectives, shards(): lax.all_to_all(request_table, 'dp', split_axis=0, concat_axis=0, tiled=True)  9.49 us
  transfers between devices with their start and end apart: 3, of which 2 were waited for; matrix products, arithmetic and copies ran while one was open for 7% of the time, Pallas kernels for 0%

commit v1 on v0

--- a/solution.py
+++ b/solution.py
@@ -4,6 +4,27 @@
 from jax.sharding import PartitionSpec as P
 
 HD = 128
+
+
+def ring_gather(value, axis, dim):
+    count, index, rows = (lax.axis_size(axis), lax.axis_index(axis), value.shape[dim])
+    right = [(i, (i + 1) % count) for i in range(count)]
+    left = [(i, (i - 1) % count) for i in range(count)]
+    out = jnp.zeros((*value.shape[:dim], count * rows, *value.shape[dim + 1 :]), value.dtype)
+    out = lax.dynamic_update_slice_in_dim(out, value, index * rows, axis=dim)
+    from_left = from_right = value
+    half = count // 2
+    for step in range(1, half + 1):
+        from_left = lax.ppermute(from_left, axis, right)
+        out = lax.dynamic_update_slice_in_dim(
+            out, from_left, (index - step) % count * rows, axis=dim
+        )
+        if step < count - half:
+            from_right = lax.ppermute(from_right, axis, left)
+            out = lax.dynamic_update_slice_in_dim(
+                out, from_right, (index + step) % count * rows, axis=dim
+            )
+    return out
 
 
 def attend(query_rows, key_rows, value_rows, heads_count, group_len):
@@ -69,9 +90,7 @@
         owners * capacity + slot_rank,
         axis=0,
     )
-    assembled = lax.all_gather(neighbour_rows, "tensor", axis=2, tiled=True).reshape(
-        per_reader * ret_len, -1
-    )
+    assembled = ring_gather(neighbour_rows, "tensor", 2).reshape(per_reader * ret_len, -1)
     key_sum = jnp.dot(assembled, w_key, preferred_element_type=jnp.float32)
     value_sum = jnp.dot(assembled, w_value, preferred_element_type=jnp.float32)
     key_rows = key_sum.astype(jnp.bfloat16)

time: 294 us -> 372 us (1.27)
  starting transfers between devices: 4.6 us -> 43.2 us
  local copies, waits for them, and re-layouts: 14.6 us -> 50.2 us
  waiting for transfers between devices: 166 us -> 181 us
  blocking collectives: 55.3 us -> 46.9 us
    ppermute x0 -> x15, waiting for transfers between devices: none -> 131 us  [the longest x8 131 us: ring_gather(): from_left = lax.ppermute(from_left, axis, right)]
    all_gather x1 -> x0, waiting for transfers between devices: 116 us -> none  [shards(): lax.all_gather(neighbour_rows, 'tensor', axis=2, tiled=True)]
    ppermute x0 -> x15, starting transfers between devices: none -> 38.5 us  [the longest x7 37 us: ring_gather(): from_right = lax.ppermute(from_right, axis, left)]
    dynamic_update_slice x0 -> x15, local copies, waits for them, and re-layouts: none -> 29.8 us  [the longest x7 15 us: ring_gather(): lax.dynamic_update_slice_in_dim(out, from_right, (index + step) % count *...]
    all_to_all x1, blocking collectives: 45.8 us -> 37.4 us  [shards(): lax.all_to_all(partial_out.reshape(live_rows, tensor_count, -1), 'tensor'...]
    broadcast_in_dim x0 -> x1, local copies, waits for them, and re-layouts: none -> 6.01 us  [ring_gather(): jnp.zeros((*value.shape[:dim], count * rows, *value.shape[dim + 1:]), val...]
  transfers between devices with their start and end apart: 3 -> 17, of which waited for: 2 -> 9; matrix products, arithmetic and copies ran while one was open for 7% -> 12% of each run, Pallas kernels for 0% -> 0%
where the time goes in v1:
time: 372 us; the launch traced here: 371 us
  waiting for transfers between devices  181 us (49%)
  local copies, waits for them, and re-layouts  50.2 us (13%)
  blocking collectives  46.9 us (13%)
  starting transfers between devices  43.2 us (12%)
  matrix products  28.8 us (8%)
  between operations  13.7 us (4%)
  other arithmetic  7.89 us (2%)
    ppermute x8, waiting for transfers between devices, ring_gather(): from_left = lax.ppermute(from_left, axis, right)  131 us
    all_to_all x1, waiting for transfers between devices, shards(): lax.all_to_all(outgoing, 'dp', split_axis=0, concat_axis=0, tiled=True)  48.8 us
    all_to_all x1, blocking collectives, shards(): lax.all_to_all(partial_out.reshape(live_rows, tensor_count, -1), 'tensor'...  37.4 us
    ppermute x7, starting transfers between devices, ring_gather(): from_right = lax.ppermute(from_right, axis, left)  37 us
    dynamic_update_slice x7, local copies, waits for them, and re-layouts, ring_gather(): lax.dynamic_update_slice_in_dim(out, from_right, (index + step) % count *...  15 us
    dynamic_update_slice x8, local copies, waits for them, and re-layouts, ring_gather(): lax.dynamic_update_slice_in_dim(out, from_left, (index - step) % count *...  14.8 us
    dot_general x1, matrix products, shards(): value_sum = jnp.dot(assembled, w_value, preferred_element_type=jnp.float32)  11.5 us
    all_to_all x1, blocking collectives, shards(): lax.all_to_all(request_table, 'dp', split_axis=0, concat_axis=0, tiled=True)  9.49 us
  transfers between devices with their start and end apart: 17, of which 9 were waited for; matrix products, arithmetic and copies ran while one was open for 12% of the time, Pallas kernels for 0%

profile of v1, /device:TPU:0, one launch (start us, length us, event | category | flops | bytes accessed | tf_op | source)
XLA Modules:
  0.0 371.4 jit_solution(13611403269802943295)
XLA Ops:
  6.5 0.8 copy.33
  7.3 0.1 reshape.302
  7.4 0.2 convert_reduce_fusion
  7.7 0.1 select_reduce_fusion
  7.8 9.5 %all_to_all.19 = s32[8,1,4]{2,1,0:T(1,128)S(1)} all-to-all(s32[8,1,4]{2,1,0:T(1,128)S(1)} %copy.34), channel_id=1, replica_groups=mesh['dp'=8,'tensor'=16] {'dp'}, dimensions={0} | all-to-all | bytes 256 | tf_op jit(solution)/shard_map/all_to_all | solution.py:83
  17.3 0.5 broadcast.334
  17.8 0.7 reduce.4
  18.7 0.1 copy.36
  18.8 5.0 %gather_fusion = bf16[32,128,512]{2,1,0:T(8,128)(2,1)} fusion(bf16[32,128,512]{2,1,0:T(8,128)(2,1)} %param.9, s32[1024]{0:T(1024)S(1)} %pad_clamp_fusion.1), kind=kCustom, calls=%fused_computation | custom fusion | bytes 8388736 | tf_op jit(solution)/shard_map/jit(_take)/gather | solution.py:84
  23.8 4.6 %broadcast_select_fusion = bf16[8,4,128,512]{3,2,1,0:T(8,128)(2,1)} fusion(bf16[8,4,128,512]{3,2,1,0:T(8,128)(2,1)} %bitcast.36, pred[8,4]{1,0:T(8,128)(4,1)S(1)} %copy.36), kind=kLoop, calls=%fused_computation.4 | loop fusion | flops 2097152 | bytes 8388640 | tf_op jit(solution)/shard_map/jit(_take)/select_n | solution.py:84
  28.4 4.6 %all-to-all-start.1 = ((bf16[8,4,128,512]{3,2,1,0:T(8,128)(2,1)}), bf16[8,4,128,512]{3,2,1,0:T(8,128)(2,1)}, u32[]{:S(2)}, u32[]{:S(2)}) async-start(bf16[8,4,128,512]{3,2,1,0:T(8,128)(2,1)} %broadcast_select_fusion), calls=%async_computation.1 | async-start | bytes 8388608 | tf_op jit(solution)/shard_map/all_to_all | solution.py:87
  33.0 0.7 all-gather.2.cloned.1.call-update
  33.7 0.1 reshape.306
  33.8 48.8 %all-to-all-done.1 = bf16[8,4,128,512]{3,2,1,0:T(8,128)(2,1)} async-done(((bf16[8,4,128,512]{3,2,1,0:T(8,128)(2,1)}), bf16[8,4,128,512]{3,2,1,0:T(8,128)(2,1)}, u32[]{:S(2)}, u32[]{:S(2)}) %all-to-all-start.1) | async-done | bytes 4194336 | tf_op jit(solution)/shard_map/all_to_all | solution.py:87
  82.6 2.8 gather_fusion.1
  85.4 6.0 %broadcast_in_dim.19 = bf16[8,128,8192]{2,1,0:T(8,128)(2,1)} broadcast(bf16[]{:T(256)} %constant.144.clone.1), dimensions={} | broadcast | bytes 16777218 | tf_op jit(solution)/shard_map/broadcast_in_dim | solution.py:13
  91.4 1.4 constant_dynamic-update-slice_fusion.15
  92.8 1.5 collective-permute-start
  94.4 4.9 %collective-permute-start.1 = (bf16[8,128,512]{2,1,0:T(8,128)(2,1)S(1)}, bf16[8,128,512]{2,1,0:T(8,128)(2,1)S(1)}, u32[]{:S(2)}, u32[]{:S(2)}) collective-permute-start(bf16[8,128,512]{2,1,0:T(8,128)(2,1)S(1)} %get-tuple-element.6), channel_id=1, source_target_pairs={{0,15},{1,0},{2,1},{3,2},{4,3},{5,4},{6,5},{7,6},{8,7},{9,8},{10,9... | collective-permute-start | bytes 3145736 | tf_op jit(solution)/shard_map/ppermute | solution.py:23
  99.3 22.9 %collective-permute-done = bf16[8,128,512]{2,1,0:T(8,128)(2,1)S(1)} collective-permute-done((bf16[8,128,512]{2,1,0:T(8,128)(2,1)S(1)}, bf16[8,128,512]{2,1,0:T(8,128)(2,1)S(1)}, u32[]{:S(2)}, u32[]{:S(2)}) %collective-permute-start) | collective-permute-done | bytes 1048608 | tf_op jit(solution)/shard_map/ppermute | solution.py:18
  122.2 5.3 %collective-permute-start.3 = (bf16[8,128,512]{2,1,0:T(8,128)(2,1)S(1)}, bf16[8,128,512]{2,1,0:T(8,128)(2,1)S(1)}, u32[]{:S(2)}, u32[]{:S(2)}) collective-permute-start(bf16[8,128,512]{2,1,0:T(8,128)(2,1)S(1)} %collective-permute-done.1), channel_id=1, source_target_pairs={{0,15},{1,0},{2,1},{3,2},{4,3},{5,4},{6,5},{7,6},{8,7},{9,8},{10,9... | collective-permute-start | bytes 3145736 | tf_op jit(solution)/shard_map/ppermute | solution.py:23
  127.5 22.0 %collective-permute-done.2 = bf16[8,128,512]{2,1,0:T(8,128)(2,1)S(1)} collective-permute-done((bf16[8,128,512]{2,1,0:T(8,128)(2,1)S(1)}, bf16[8,128,512]{2,1,0:T(8,128)(2,1)S(1)}, u32[]{:S(2)}, u32[]{:S(2)}) %collective-permute-start.2) | collective-permute-done | bytes 1048608 | tf_op jit(solution)/shard_map/ppermute | solution.py:18
  149.5 5.3 %collective-permute-start.5 = (bf16[8,128,512]{2,1,0:T(8,128)(2,1)S(1)}, bf16[8,128,512]{2,1,0:T(8,128)(2,1)S(1)}, u32[]{:S(2)}, u32[]{:S(2)}) collective-permute-start(bf16[8,128,512]{2,1,0:T(8,128)(2,1)S(1)} %collective-permute-done.3), channel_id=1, source_target_pairs={{0,15},{1,0},{2,1},{3,2},{4,3},{5,4},{6,5},{7,6},{8,7},{9,8},{10,9... | collective-permute-start | bytes 3145736 | tf_op jit(solution)/shard_map/ppermute | solution.py:23
  154.9 21.2 %collective-permute-done.4 = bf16[8,128,512]{2,1,0:T(8,128)(2,1)S(1)} collective-permute-done((bf16[8,128,512]{2,1,0:T(8,128)(2,1)S(1)}, bf16[8,128,512]{2,1,0:T(8,128)(2,1)S(1)}, u32[]{:S(2)}, u32[]{:S(2)}) %collective-permute-start.4) | collective-permute-done | bytes 1048608 | tf_op jit(solution)/shard_map/ppermute | solution.py:18
  176.0 5.3 %collective-permute-start.7 = (bf16[8,128,512]{2,1,0:T(8,128)(2,1)S(1)}, bf16[8,128,512]{2,1,0:T(8,128)(2,1)S(1)}, u32[]{:S(2)}, u32[]{:S(2)}) collective-permute-start(bf16[8,128,512]{2,1,0:T(8,128)(2,1)S(1)} %collective-permute-done.5), channel_id=1, source_target_pairs={{0,15},{1,0},{2,1},{3,2},{4,3},{5,4},{6,5},{7,6},{8,7},{9,8},{10,9... | collective-permute-start | bytes 3145736 | tf_op jit(solution)/shard_map/ppermute | solution.py:23
  181.4 20.3 %collective-permute-done.6 = bf16[8,128,512]{2,1,0:T(8,128)(2,1)S(1)} collective-permute-done((bf16[8,128,512]{2,1,0:T(8,128)(2,1)S(1)}, bf16[8,128,512]{2,1,0:T(8,128)(2,1)S(1)}, u32[]{:S(2)}, u32[]{:S(2)}) %collective-permute-start.6) | collective-permute-done | bytes 1048608 | tf_op jit(solution)/shard_map/ppermute | solution.py:18
  201.7 5.3 %collective-permute-start.9 = (bf16[8,128,512]{2,1,0:T(8,128)(2,1)S(1)}, bf16[8,128,512]{2,1,0:T(8,128)(2,1)}, u32[]{:S(2)}, u32[]{:S(2)}) collective-permute-start(bf16[8,128,512]{2,1,0:T(8,128)(2,1)S(1)} %collective-permute-done.7), channel_id=1, source_target_pairs={{0,15},{1,0},{2,1},{3,2},{4,3},{5,4},{6,5},{7,6},{8,7},{9,8},{10,9... | collective-permute-start | bytes 3145736 | tf_op jit(solution)/shard_map/ppermute | solution.py:23
  207.0 19.4 %collective-permute-done.8 = bf16[8,128,512]{2,1,0:T(8,128)(2,1)S(1)} collective-permute-done((bf16[8,128,512]{2,1,0:T(8,128)(2,1)S(1)}, bf16[8,128,512]{2,1,0:T(8,128)(2,1)S(1)}, u32[]{:S(2)}, u32[]{:S(2)}) %collective-permute-start.8) | collective-permute-done | bytes 1048608 | tf_op jit(solution)/shard_map/ppermute | solution.py:18
  226.5 5.4 %collective-permute-start.11 = (bf16[8,128,512]{2,1,0:T(8,128)(2,1)}, bf16[8,128,512]{2,1,0:T(8,128)(2,1)}, u32[]{:S(2)}, u32[]{:S(2)}) collective-permute-start(bf16[8,128,512]{2,1,0:T(8,128)(2,1)} %collective-permute-done.9), channel_id=1, source_target_pairs={{0,15},{1,0},{2,1},{3,2},{4,3},{5,4},{6,5},{7,6},{8,7},{9,8},{10,9... | collective-permute-start | bytes 3145736 | tf_op jit(solution)/shard_map/ppermute | solution.py:23
  231.9 2.3 constant_dynamic-update-slice_fusion.14
  234.3 2.3 constant_dynamic-update-slice_fusion.13
  236.6 13.9 %collective-permute-done.10 = bf16[8,128,512]{2,1,0:T(8,128)(2,1)} collective-permute-done((bf16[8,128,512]{2,1,0:T(8,128)(2,1)S(1)}, bf16[8,128,512]{2,1,0:T(8,128)(2,1)}, u32[]{:S(2)}, u32[]{:S(2)}) %collective-permute-start.10) | collective-permute-done | bytes 1048608 | tf_op jit(solution)/shard_map/ppermute | solution.py:18
  250.5 2.3 constant_dynamic-update-slice_fusion.12
  252.9 2.3 constant_dynamic-update-slice_fusion.11
  255.2 2.3 constant_dynamic-update-slice_fusion.10
  257.5 2.3 constant_dynamic-update-slice_fusion.9
  259.8 5.3 %collective-permute-start.13 = (bf16[8,128,512]{2,1,0:T(8,128)(2,1)}, bf16[8,128,512]{2,1,0:T(8,128)(2,1)}, u32[]{:S(2)}, u32[]{:S(2)}) collective-permute-start(bf16[8,128,512]{2,1,0:T(8,128)(2,1)} %collective-permute-done.11), channel_id=1, source_target_pairs={{0,15},{1,0},{2,1},{3,2},{4,3},{5,4},{6,5},{7,6},{8,7},{9,8},{10,9... | collective-permute-start | bytes 3145736 | tf_op jit(solution)/shard_map/ppermute | solution.py:23
  265.1 4.7 %fusion.14 = bf16[256,256]{1,0:T(8,128)(2,1)S(1)} fusion(bf16[256,8192]{1,0:T(8,128)(2,1)} %all-gather.2.cloned.1.call-done, bf16[8192,256]{1,0:T(8,128)(2,1)} %param.10), kind=kOutput, calls=%fused_computation.65 | convolution fusion | flops 1073741824 | bytes 8519680 | tf_op jit(solution)/shard_map/dot_general | solution.py:66
  270.0 4.0 %collective-permute-done.12 = bf16[8,128,512]{2,1,0:T(8,128)(2,1)} collective-permute-done((bf16[8,128,512]{2,1,0:T(8,128)(2,1)}, bf16[8,128,512]{2,1,0:T(8,128)(2,1)}, u32[]{:S(2)}, u32[]{:S(2)}) %collective-permute-start.12) | collective-permute-done | bytes 1048608 | tf_op jit(solution)/shard_map/ppermute | solution.py:18
  273.9 1.1 constant_dynamic-update-slice_fusion.8
  275.0 1.2 constant_dynamic-update-slice_fusion.7
  276.2 1.1 constant_dynamic-update-slice_fusion.6
  277.3 2.3 constant_dynamic-update-slice_fusion.5
  279.6 2.3 constant_dynamic-update-slice_fusion.4
  281.9 2.3 constant_dynamic-update-slice_fusion.3
  284.2 2.3 constant_dynamic-update-slice_fusion.2
  286.5 2.3 constant_dynamic-update-slice_fusion.1
  288.7 7.6 %collective-permute-done.14 = bf16[8,128,512]{2,1,0:T(8,128)(2,1)S(1)} collective-permute-done((bf16[8,128,512]{2,1,0:T(8,128)(2,1)}, bf16[8,128,512]{2,1,0:T(8,128)(2,1)S(1)}, u32[]{:S(2)}, u32[]{:S(2)}) %collective-permute-start.14) | collective-permute-done | bytes 1048608 | tf_op jit(solution)/shard_map/ppermute | solution.py:18
  296.4 1.1 constant_dynamic-update-slice_fusion
  297.5 8.2 %convolution_convert_fusion.1 = bf16[1024,256]{1,0:T(8,128)(2,1)S(1)} fusion(bf16[1024,8192]{1,0:T(8,128)(2,1)} %bitcast.7, bf16[8192,256]{1,0:T(8,128)(2,1)S(1)} %copy-done.6), kind=kOutput, calls=%fused_computation.5 | convolution fusion | flops 4295229440 | bytes 21495808 | tf_op jit(solution)/shard_map/dot_general | solution.py:94
  305.7 0.1 reshape.310
  305.8 0.3 convolution_multiply_fusion
  306.1 0.3 fusion.13
  306.4 11.5 %convolution_convert_fusion.2 = bf16[1024,256]{1,0:T(8,128)(2,1)S(1)} fusion(bf16[1024,8192]{1,0:T(8,128)(2,1)} %bitcast.7, bf16[8192,256]{1,0:T(8,128)(2,1)} %param.12), kind=kOutput, calls=%fused_computation.6 | convolution fusion | flops 4295229440 | bytes 21495808 | tf_op jit(solution)/shard_map/dot_general | solution.py:95
  317.8 0.1 reshape.308
  317.9 1.0 fusion.3
  318.9 0.1 copy.41
  319.1 3.2 convolution_convert_fusion
  322.3 1.5 copy.44
  323.8 0.3 slice.14
  324.1 1.8 copy.42
  325.9 37.4 %all_to_all.20 = bf16[193,16,512]{2,0,1:T(8,128)(2,1)S(1)} all-to-all(bf16[193,16,512]{2,0,1:T(8,128)(2,1)S(1)} %copy.42), channel_id=1, replica_groups=mesh['dp'=8,'tensor'=16] {'tensor'}, dimensions={1} | all-to-all | bytes 6324224 | tf_op jit(solution)/shard_map/all_to_all | solution.py:104
  363.3 0.5 reduce_sum.45
  363.8 0.8 concatenate.7
  (46 shorter events, 0.6 us)
Async XLA Ops:
  28.4 54.2 %all-to-all-start.1 = ((bf16[8,4,128,512]{3,2,1,0:T(8,128)(2,1)}), bf16[8,4,128,512]{3,2,1,0:T(8,128)(2,1)}, u32[]{:S(2)}, u32[]{:S(2)}) async-start(bf16[8,4,128,512]{3,2,1,0:T(8,128)(2,1)} %broadcast_select_fusion), calls=%async_computation.1 | async-start | bytes 8388608 | tf_op jit(solution)/shard_map/all_to_all | solution.py:87
  33.0 232.2 %all-gather.2.cloned.1.call-start = ((), (), s32[]{:S(2)}) async-start(), calls=%async_computation.3 | async-start | bytes 4456448 | tf_op jit(solution)/shard_map/all_gather | solution.py:67
  92.8 29.3 %collective-permute-start = (bf16[8,128,512]{2,1,0:T(8,128)(2,1)S(1)}, bf16[8,128,512]{2,1,0:T(8,128)(2,1)S(1)}, u32[]{:S(2)}, u32[]{:S(2)}) collective-permute-start(bf16[8,128,512]{2,1,0:T(8,128)(2,1)S(1)} %get-tuple-element.6), channel_id=1, source_target_pairs={{0,1},{1,2},{2,3},{3,4},{4,5},{5,6},{6,7},{7,8},{8,9},{9,10},{10,1... | collective-permute-start | bytes 3145736 | tf_op jit(solution)/shard_map/ppermute | solution.py:18
  94.4 27.8 %collective-permute-start.1 = (bf16[8,128,512]{2,1,0:T(8,128)(2,1)S(1)}, bf16[8,128,512]{2,1,0:T(8,128)(2,1)S(1)}, u32[]{:S(2)}, u32[]{:S(2)}) collective-permute-start(bf16[8,128,512]{2,1,0:T(8,128)(2,1)S(1)} %get-tuple-element.6), channel_id=1, source_target_pairs={{0,15},{1,0},{2,1},{3,2},{4,3},{5,4},{6,5},{7,6},{8,7},{9,8},{10,9... | collective-permute-start | bytes 3145736 | tf_op jit(solution)/shard_map/ppermute | solution.py:23
  122.1 104.3 %copy-start.1 = (bf16[8,128,512]{2,1,0:T(8,128)(2,1)}, bf16[8,128,512]{2,1,0:T(8,128)(2,1)S(1)}, u32[]{:S(2)}) copy-start(bf16[8,128,512]{2,1,0:T(8,128)(2,1)S(1)} %collective-permute-done) | copy-start | bytes 3145732
  122.2 27.4 %collective-permute-start.2 = (bf16[8,128,512]{2,1,0:T(8,128)(2,1)S(1)}, bf16[8,128,512]{2,1,0:T(8,128)(2,1)S(1)}, u32[]{:S(2)}, u32[]{:S(2)}) collective-permute-start(bf16[8,128,512]{2,1,0:T(8,128)(2,1)S(1)} %collective-permute-done), channel_id=1, source_target_pairs={{0,1},{1,2},{2,3},{3,4},{4,5},{5,6},{6,7},{7,8},{8,9},{9,10},{10,1... | collective-permute-start | bytes 3145736 | tf_op jit(solution)/shard_map/ppermute | solution.py:18
  122.2 104.3 %copy-start.2 = (bf16[8,128,512]{2,1,0:T(8,128)(2,1)}, bf16[8,128,512]{2,1,0:T(8,128)(2,1)S(1)}, u32[]{:S(2)}) copy-start(bf16[8,128,512]{2,1,0:T(8,128)(2,1)S(1)} %collective-permute-done.1) | copy-start | bytes 3145732
  122.2 27.4 %collective-permute-start.3 = (bf16[8,128,512]{2,1,0:T(8,128)(2,1)S(1)}, bf16[8,128,512]{2,1,0:T(8,128)(2,1)S(1)}, u32[]{:S(2)}, u32[]{:S(2)}) collective-permute-start(bf16[8,128,512]{2,1,0:T(8,128)(2,1)S(1)} %collective-permute-done.1), channel_id=1, source_target_pairs={{0,15},{1,0},{2,1},{3,2},{4,3},{5,4},{6,5},{7,6},{8,7},{9,8},{10,9... | collective-permute-start | bytes 3145736 | tf_op jit(solution)/shard_map/ppermute | solution.py:23
  149.5 77.0 %copy-start = (bf16[8,128,512]{2,1,0:T(8,128)(2,1)}, bf16[8,128,512]{2,1,0:T(8,128)(2,1)S(1)}, u32[]{:S(2)}) copy-start(bf16[8,128,512]{2,1,0:T(8,128)(2,1)S(1)} %collective-permute-done.2) | copy-start | bytes 3145732
  149.5 26.5 %collective-permute-start.4 = (bf16[8,128,512]{2,1,0:T(8,128)(2,1)S(1)}, bf16[8,128,512]{2,1,0:T(8,128)(2,1)S(1)}, u32[]{:S(2)}, u32[]{:S(2)}) collective-permute-start(bf16[8,128,512]{2,1,0:T(8,128)(2,1)S(1)} %collective-permute-done.2), channel_id=1, source_target_pairs={{0,1},{1,2},{2,3},{3,4},{4,5},{5,6},{6,7},{7,8},{8,9},{9,10},{10,1... | collective-permute-start | bytes 3145736 | tf_op jit(solution)/shard_map/ppermute | solution.py:18
  149.5 77.0 %copy-start.3 = (bf16[8,128,512]{2,1,0:T(8,128)(2,1)}, bf16[8,128,512]{2,1,0:T(8,128)(2,1)S(1)}, u32[]{:S(2)}) copy-start(bf16[8,128,512]{2,1,0:T(8,128)(2,1)S(1)} %collective-permute-done.3) | copy-start | bytes 3145732
  149.5 26.5 %collective-permute-start.5 = (bf16[8,128,512]{2,1,0:T(8,128)(2,1)S(1)}, bf16[8,128,512]{2,1,0:T(8,128)(2,1)S(1)}, u32[]{:S(2)}, u32[]{:S(2)}) collective-permute-start(bf16[8,128,512]{2,1,0:T(8,128)(2,1)S(1)} %collective-permute-done.3), channel_id=1, source_target_pairs={{0,15},{1,0},{2,1},{3,2},{4,3},{5,4},{6,5},{7,6},{8,7},{9,8},{10,9... | collective-permute-start | bytes 3145736 | tf_op jit(solution)/shard_map/ppermute | solution.py:23
  176.0 50.5 %copy-start.4 = (bf16[8,128,512]{2,1,0:T(8,128)(2,1)}, bf16[8,128,512]{2,1,0:T(8,128)(2,1)S(1)}, u32[]{:S(2)}) copy-start(bf16[8,128,512]{2,1,0:T(8,128)(2,1)S(1)} %collective-permute-done.4) | copy-start | bytes 3145732
  176.0 25.7 %collective-permute-start.6 = (bf16[8,128,512]{2,1,0:T(8,128)(2,1)S(1)}, bf16[8,128,512]{2,1,0:T(8,128)(2,1)S(1)}, u32[]{:S(2)}, u32[]{:S(2)}) collective-permute-start(bf16[8,128,512]{2,1,0:T(8,128)(2,1)S(1)} %collective-permute-done.4), channel_id=1, source_target_pairs={{0,1},{1,2},{2,3},{3,4},{4,5},{5,6},{6,7},{7,8},{8,9},{9,10},{10,1... | collective-permute-start | bytes 3145736 | tf_op jit(solution)/shard_map/ppermute | solution.py:18
  176.0 50.5 %copy-start.5 = (bf16[8,128,512]{2,1,0:T(8,128)(2,1)}, bf16[8,128,512]{2,1,0:T(8,128)(2,1)S(1)}, u32[]{:S(2)}) copy-start(bf16[8,128,512]{2,1,0:T(8,128)(2,1)S(1)} %collective-permute-done.5) | copy-start | bytes 3145732
  176.0 25.6 %collective-permute-start.7 = (bf16[8,128,512]{2,1,0:T(8,128)(2,1)S(1)}, bf16[8,128,512]{2,1,0:T(8,128)(2,1)S(1)}, u32[]{:S(2)}, u32[]{:S(2)}) collective-permute-start(bf16[8,128,512]{2,1,0:T(8,128)(2,1)S(1)} %collective-permute-done.5), channel_id=1, source_target_pairs={{0,15},{1,0},{2,1},{3,2},{4,3},{5,4},{6,5},{7,6},{8,7},{9,8},{10,9... | collective-permute-start | bytes 3145736 | tf_op jit(solution)/shard_map/ppermute | solution.py:23
  201.7 24.8 %collective-permute-start.8 = (bf16[8,128,512]{2,1,0:T(8,128)(2,1)S(1)}, bf16[8,128,512]{2,1,0:T(8,128)(2,1)S(1)}, u32[]{:S(2)}, u32[]{:S(2)}) collective-permute-start(bf16[8,128,512]{2,1,0:T(8,128)(2,1)S(1)} %collective-permute-done.6), channel_id=1, source_target_pairs={{0,1},{1,2},{2,3},{3,4},{4,5},{5,6},{6,7},{7,8},{8,9},{9,10},{10,1... | collective-permute-start | bytes 3145736 | tf_op jit(solution)/shard_map/ppermute | solution.py:18
  201.7 24.8 %collective-permute-start.9 = (bf16[8,128,512]{2,1,0:T(8,128)(2,1)S(1)}, bf16[8,128,512]{2,1,0:T(8,128)(2,1)}, u32[]{:S(2)}, u32[]{:S(2)}) collective-permute-start(bf16[8,128,512]{2,1,0:T(8,128)(2,1)S(1)} %collective-permute-done.7), channel_id=1, source_target_pairs={{0,15},{1,0},{2,1},{3,2},{4,3},{5,4},{6,5},{7,6},{8,7},{9,8},{10,9... | collective-permute-start | bytes 3145736 | tf_op jit(solution)/shard_map/ppermute | solution.py:23
  226.5 24.0 %collective-permute-start.10 = (bf16[8,128,512]{2,1,0:T(8,128)(2,1)S(1)}, bf16[8,128,512]{2,1,0:T(8,128)(2,1)}, u32[]{:S(2)}, u32[]{:S(2)}) collective-permute-start(bf16[8,128,512]{2,1,0:T(8,128)(2,1)S(1)} %collective-permute-done.8), channel_id=1, source_target_pairs={{0,1},{1,2},{2,3},{3,4},{4,5},{5,6},{6,7},{7,8},{8,9},{9,10},{10,1... | collective-permute-start | bytes 3145736 | tf_op jit(solution)/shard_map/ppermute | solution.py:18
  226.5 33.2 %collective-permute-start.11 = (bf16[8,128,512]{2,1,0:T(8,128)(2,1)}, bf16[8,128,512]{2,1,0:T(8,128)(2,1)}, u32[]{:S(2)}, u32[]{:S(2)}) collective-permute-start(bf16[8,128,512]{2,1,0:T(8,128)(2,1)} %collective-permute-done.9), channel_id=1, source_target_pairs={{0,15},{1,0},{2,1},{3,2},{4,3},{5,4},{6,5},{7,6},{8,7},{9,8},{10,9... | collective-permute-start | bytes 3145736 | tf_op jit(solution)/shard_map/ppermute | solution.py:23
  250.5 23.4 %collective-permute-start.12 = (bf16[8,128,512]{2,1,0:T(8,128)(2,1)}, bf16[8,128,512]{2,1,0:T(8,128)(2,1)}, u32[]{:S(2)}, u32[]{:S(2)}) collective-permute-start(bf16[8,128,512]{2,1,0:T(8,128)(2,1)} %collective-permute-done.10), channel_id=1, source_target_pairs={{0,1},{1,2},{2,3},{3,4},{4,5},{5,6},{6,7},{7,8},{8,9},{9,10},{10,1... | collective-permute-start | bytes 3145736 | tf_op jit(solution)/shard_map/ppermute | solution.py:18
  259.8 26.7 %collective-permute-start.13 = (bf16[8,128,512]{2,1,0:T(8,128)(2,1)}, bf16[8,128,512]{2,1,0:T(8,128)(2,1)}, u32[]{:S(2)}, u32[]{:S(2)}) collective-permute-start(bf16[8,128,512]{2,1,0:T(8,128)(2,1)} %collective-permute-done.11), channel_id=1, source_target_pairs={{0,15},{1,0},{2,1},{3,2},{4,3},{5,4},{6,5},{7,6},{8,7},{9,8},{10,9... | collective-permute-start | bytes 3145736 | tf_op jit(solution)/shard_map/ppermute | solution.py:23
  269.9 27.5 %copy-start.6 = (bf16[8192,256]{1,0:T(8,128)(2,1)S(1)}, bf16[8192,256]{1,0:T(8,128)(2,1)}, u32[]{:S(2)}) copy-start(bf16[8192,256]{1,0:T(8,128)(2,1)} %param.11) | copy-start | bytes 12582916
  273.9 22.4 %collective-permute-start.14 = (bf16[8,128,512]{2,1,0:T(8,128)(2,1)}, bf16[8,128,512]{2,1,0:T(8,128)(2,1)S(1)}, u32[]{:S(2)}, u32[]{:S(2)}) collective-permute-start(bf16[8,128,512]{2,1,0:T(8,128)(2,1)} %collective-permute-done.12), channel_id=1, source_target_pairs={{0,1},{1,2},{2,3},{3,4},{4,5},{5,6},{6,7},{7,8},{8,9},{9,10},{10,1... | collective-permute-start | bytes 3145736 | tf_op jit(solution)/shard_map/ppermute | solution.py:18
Sparse Core Ops, SparseCore 0:
  35.9 59.7 all-gather.1
